TPU v7x, 128 devices: a whole 4x4x4 slice. The times are simulated.
128 devices in a mesh: dp: 16 (over x, y_lo, core), tensor: 8 (over z, y_hi).
Axes of the slice: x: 4, y: 4 (y_hi: 2, y_lo: 2; y = y_hi * 2 + y_lo), z: 4, core: 2. Of those that a mesh axis runs over, the one named last changes fastest.
Arguments:
- rows_in: bfloat16 [2048, 6144], P('dp'), may hold values from -6 to 6
- out_grad: bfloat16 [2048, 6144], P('dp'), may hold values from -1.5 to 1.5
- gate_pre: bfloat16 [2048, 12288], P('dp', 'tensor'), may hold values from -5 to 5
- up_pre: bfloat16 [2048, 12288], P('dp', 'tensor'), may hold values from -5 to 5
- w_gate: bfloat16 [2, 6144, 12288], P(None, 'dp', 'tensor'), may hold values from -0.078125 to 0.078125
- w_up: bfloat16 [2, 6144, 12288], P(None, 'dp', 'tensor'), may hold values from -0.078125 to 0.078125
- w_down: bfloat16 [2, 12288, 6144], P(None, 'tensor', 'dp'), may hold values from -0.0546875 to 0.0546875
- live_rows: int32 [16], P('dp'), may hold values from 32 to 128, as said below
- block_expert: int32 [16], replicated, may hold values from 0 to 1, as said below
Outputs:
- input_grad: bfloat16 [2048, 6144], P('dp', 'tensor')
- grad_gate: bfloat16 [2, 6144, 12288], P(None, 'dp', 'tensor')
- grad_up: bfloat16 [2, 6144, 12288], P(None, 'dp', 'tensor')
- grad_down: bfloat16 [2, 12288, 6144], P(None, 'tensor', 'dp')
Inputs may be any that keep to these rules, and one draw needn't show every extreme that they name: `live_rows`: entry k counts the live rows among rank k's 128 rows; they come first and the rest are padding; some rank is full. `block_expert`: the expert of each aligned block of 128 rows; every expert owns at least one block.
All inputs are finite; a program needn't handle non-finite values.
Results may differ from a plain program's by a relative error of at most 0.005.
Values may be sent and summed in bfloat16 or wider, within the bound.
No kernel may reach another device: no remote copies, remote signals or barrier semaphores. Data moves between devices by JAX's collectives and lax.ppermute only.
A program may use at most 128 MiB of HBM per device.

v0:
```python
import numpy as np
import jax
import jax.numpy as jnp
from jax import lax
from jax.sharding import Mesh
from jax.sharding import PartitionSpec as P

BLOCK = 128
AXES = ("x", "ylo", "core", "z", "yhi")
SIZES = (4, 2, 2, 4, 2)
DP = ("x", "ylo", "core")
TP = ("z", "yhi")
CHIPS = ("x", "ylo")
N_DP = 16
N_TP = 8


def rank_of_pos(pos):
    core, x, ylo = (pos // 8, pos % 8 // 2, pos % 2)
    return x * 4 + ylo * 2 + core


POS_RANK = np.array([rank_of_pos(p) for p in range(N_DP)], np.int32)


def deliver_perm(k):
    pairs = []
    for i in range(N_DP):
        for t in range(N_TP):
            dest = rank_of_pos(2 * t + (i % 2 ^ k))
            pairs.append((i * N_TP + t, dest * N_TP + i // 2))
    return pairs


def contract_rows(left_op, right_op):
    return lax.dot_general(
        left_op, right_op, (((0,), (0,)), ((), ())), preferred_element_type=jnp.float32
    )


def contract_cols(left_op, right_op):
    return lax.dot_general(
        left_op, right_op, (((1,), (1,)), ((), ())), preferred_element_type=jnp.float32
    )


def expert_masks(block_expert, row_count, expert_count):
    spread = jnp.broadcast_to(block_expert[:, None], (row_count // BLOCK, BLOCK)).reshape(
        row_count, 1
    )
    return [(spread == which).astype(jnp.bfloat16) for which in range(expert_count)]


def to_gathered_order(cols):
    width = cols.shape[1]
    return cols.reshape(4, 2, 2, BLOCK, width).transpose(2, 0, 1, 3, 4).reshape(-1, width)


def shards(rows_in, out_grad, gate_pre, up_pre, w_gate, w_up, w_down, live_rows, block_expert):
    rows_dev = rows_in.shape[0]
    expert_count = w_gate.shape[0]
    ff = gate_pre.shape[1]
    dy_cols = to_gathered_order(
        lax.all_to_all(out_grad, DP, split_axis=1, concat_axis=0, tiled=True)
    )
    x_cols = to_gathered_order(lax.all_to_all(rows_in, DP, split_axis=1, concat_axis=0, tiled=True))
    row_count = dy_cols.shape[0]
    expert_g = jnp.take(block_expert, jnp.asarray(POS_RANK), axis=0)
    masks = expert_masks(expert_g, row_count, expert_count)
    positions = jnp.arange(rows_dev, dtype=jnp.int32)[:, None]
    row_mask = (positions < live_rows[0]).astype(jnp.float32)
    gate_vals = gate_pre.astype(jnp.float32)
    up_vals = up_pre.astype(jnp.float32)
    sigmoid = jax.nn.sigmoid(gate_vals)
    silu_vals = gate_vals * sigmoid
    hidden = (silu_vals * up_vals * row_mask).astype(jnp.bfloat16)
    result = jnp.zeros((row_count, ff), jnp.float32)
    for which in range(expert_count):
        result = result + contract_cols(dy_cols * masks[which], w_down[which])
    result = lax.psum_scatter(
        result.reshape(2, row_count // 2, ff), "core", scatter_dimension=0, tiled=True
    ).reshape(row_count // 2, ff)
    hidden_grad = lax.psum_scatter(result, CHIPS, scatter_dimension=0, tiled=True)
    up_grad = (hidden_grad * silu_vals * row_mask).astype(jnp.bfloat16)
    gate_grad = (
        hidden_grad * up_vals * sigmoid * (1.0 + gate_vals * (1.0 - sigmoid)) * row_mask
    ).astype(jnp.bfloat16)
    packed = jnp.stack([hidden, gate_grad, up_grad], axis=1)
    packed = lax.all_gather(packed, CHIPS, axis=0, tiled=True)
    packed = lax.all_gather(packed, "core", axis=0, tiled=True)
    hid_g, gate_g, up_g = (packed[:, 0], packed[:, 1], packed[:, 2])
    down_terms = []
    gate_terms = []
    up_terms = []
    partial_rows = jnp.zeros((row_count, w_gate.shape[1]), jnp.float32)
    for which in range(expert_count):
        down_terms.append(contract_rows(hid_g * masks[which], dy_cols))
        gate_masked = gate_g * masks[which]
        up_masked = up_g * masks[which]
        gate_terms.append(contract_rows(x_cols, gate_masked))
        up_terms.append(contract_rows(x_cols, up_masked))
        partial_rows = (
            partial_rows
            + contract_cols(gate_masked, w_gate[which])
            + contract_cols(up_masked, w_up[which])
        )
    down_total = jnp.stack(down_terms, 0)
    gate_total = jnp.stack(gate_terms, 0)
    up_total = jnp.stack(up_terms, 0)
    width = partial_rows.shape[1]
    summed = lax.psum_scatter(
        partial_rows.reshape(N_TP, row_count // N_TP, width), TP, scatter_dimension=0, tiled=True
    ).reshape(2, rows_dev, width)
    core = lax.axis_index("core")
    ylo = lax.axis_index("ylo")
    got = []
    for k in range(2):
        piece = lax.dynamic_index_in_dim(summed, core ^ k, 0, keepdims=False)
        got.append(lax.ppermute(piece, AXES, deliver_perm(k)))
    first = jnp.where(ylo == 0, got[0], got[1])
    second = jnp.where(ylo == 0, got[1], got[0])
    input_grad = jnp.concatenate([first, second], axis=1).astype(jnp.bfloat16)
    return (
        input_grad,
        gate_total.astype(jnp.bfloat16),
        up_total.astype(jnp.bfloat16),
        down_total.astype(jnp.bfloat16),
    )


def solution(mesh):
    fine = Mesh(mesh.devices.reshape(SIZES), AXES)
    return jax.shard_map(
        shards,
        mesh=fine,
        in_specs=(
            P(DP, None),
            P(DP, None),
            P(DP, TP),
            P(DP, TP),
            P(None, DP, TP),
            P(None, DP, TP),
            P(None, TP, DP),
            P(DP),
            P(),
        ),
        out_specs=(P(DP, TP), P(None, DP, TP), P(None, DP, TP), P(None, TP, DP)),
        check_vma=False,
    )
```

profile of v0, /device:TPU:57, one launch (start us, length us, event | category | flops | bytes accessed | tf_op | source)
XLA Modules:
  0.0 575.7 jit_solution(3465949403237092074)
XLA Ops:
  7.2 2.6 copy.28
  9.8 6.2 %all-to-all-start = ((bf16[128,16,384]{0,2,1:T(8,128)(2,1)}), bf16[128,16,384]{0,2,1:T(8,128)(2,1)S(1)}, u32[]{:S(2)}, u32[]{:S(2)}) async-start(bf16[128,16,384]{0,2,1:T(8,128)(2,1)} %bitcast.2), calls=%async_computation | async-start | bytes 3145728 | tf_op jit(solution)/shard_map/all_to_all | solution.py:64
  16.1 0.7 gather_fusion
  17.2 20.2 %all-to-all-done = bf16[128,16,384]{0,2,1:T(8,128)(2,1)S(1)} async-done(((bf16[128,16,384]{0,2,1:T(8,128)(2,1)}), bf16[128,16,384]{0,2,1:T(8,128)(2,1)S(1)}, u32[]{:S(2)}, u32[]{:S(2)}) %all-to-all-start) | async-done | bytes 1572896 | tf_op jit(solution)/shard_map/all_to_all | solution.py:64
  37.4 0.9 copy.29
  38.2 0.4 broadcast_multiply_fusion
  38.6 0.2 copy.31
  38.8 0.2 copy.33
  39.0 1.4 copy-done.2
  40.5 3.5 fusion.77
  43.9 6.5 %convolution_add_fusion = f32[2048,1536]{1,0:T(8,128)} fusion(f32[2048,1536]{1,0:T(8,128)S(1)} %fusion.77, bf16[2048,384]{1,0:T(8,128)(2,1)S(1)} %bitcast.138, bf16[2,1536,384]{2,1,0:T(8,128)(2,1)S(1)} %copy-done.2), kind=kOutput, calls=%fused_computation.1 | convolution fusion | flops 2419064832 | bytes 27918336 | tf_op jit(solution)/shard_map/dot_general | solution.py:42
  50.6 25.1 %reduce-scatter.4.cloned.1.call-done = f32[1,1024,1536]{2,1,0:T(8,128)} async-done(((f32[2,1024,1536]{2,1,0:T(8,128)}), f32[1,1024,1536]{2,1,0:T(8,128)}) %reduce-scatter.4.cloned.1.call-update) | async-done | bytes 6291472 | tf_op jit(solution)/shard_map/reduce_scatter | solution.py:80
  76.4 131.5 %reduce-scatter.6.cloned.1.call-done = f32[128,1536]{1,0:T(8,128)} async-done(((f32[1024,1536]{1,0:T(8,128)}), f32[128,1536]{1,0:T(8,128)}) %reduce-scatter.6.cloned.1.call-update) | async-done | bytes 786448 | tf_op jit(solution)/shard_map/reduce_scatter | solution.py:83
  208.0 1.7 fusion.97
  209.7 1.1 pad_maximum_fusion.3
  210.9 189.0 %all-gather.3.cloned.1.call-done = bf16[1024,3,1536]{2,0,1:T(8,128)(2,1)} async-done(((bf16[128,3,1536]{2,0,1:T(8,128)(2,1)}), bf16[1024,3,1536]{2,0,1:T(8,128)(2,1)}) %all-gather.3.cloned.1.call-update) | async-done | bytes 9437200 | tf_op jit(solution)/shard_map/all_gather | solution.py:89
  399.9 1.4 copy-done.3
  401.3 1.6 copy.34
  402.9 7.1 %all-to-all-start.1 = ((bf16[128,16,384]{0,2,1:T(8,128)(2,1)}), bf16[128,16,384]{0,2,1:T(8,128)(2,1)S(1)}, u32[]{:S(2)}, u32[]{:S(2)}) async-start(bf16[128,16,384]{0,2,1:T(8,128)(2,1)} %bitcast.142), calls=%async_computation.4 | async-start | bytes 3145728 | tf_op jit(solution)/shard_map/all_to_all | solution.py:66
  410.0 0.5 reduce-scatter.8.cloned.1.call-start
  410.6 28.3 %all-gather.5.cloned.1.call-done = bf16[2048,3,1536]{2,0,1:T(8,128)(2,1)} async-done(((bf16[1024,3,1536]{2,0,1:T(8,128)(2,1)}), bf16[2048,3,1536]{2,0,1:T(8,128)(2,1)}) %all-gather.5.cloned.1.call-update) | async-done | bytes 18874384 | tf_op jit(solution)/shard_map/all_gather | solution.py:90
  438.9 8.3 %fusion.6 = f32[2048,384]{1,0:T(8,128)} fusion(bf16[2048,3,1536]{2,0,1:T(8,128)(2,1)} %all-gather.5.cloned.1.call-done, bf16[2048]{0:T(1024)(128)(2,1)S(1)} %get-tuple-element.31, bf16[2,384,1536]{2,1,0:T(8,128)(2,1)} %param.15), kind=kOutput, calls=%fused_computation.8 | convolution fusion | flops 2419064832 | bytes 10620928 | tf_op jit(solution)/shard_map/dot_general | solution.py:42
  447.3 1.3 copy-done.10
  448.6 0.7 copy-done.11
  449.2 5.2 fusion.14
  454.4 5.2 fusion.18
  459.6 7.3 %add_add_fusion = f32[2048,384]{1,0:T(8,128)} fusion(f32[2048,384]{1,0:T(8,128)} %fusion.6, f32[2048,384]{1,0:T(8,128)} %fusion.18, f32[2048,384]{1,0:T(8,128)} %fusion.14, bf16[2048,3,1536]{2,0,1:T(8,128)(2,1)S(1)} %copy-done.10, bf16[2048]{0:T(1024)(128)(2,1)S(1)} %get-tuple-element.31, bf16[2,384,1536]{2,1,0:T(8,128)(2,1)S(1)} %copy-done.12), kind=kOutput, calls=%fused_computation.30 | convolution fusion | flops 2421424128 | bytes 20058112 | tf_op jit(solution)/shard_map/dot_general | solution.py:42
  466.9 1.6 copy.36
  468.5 1.7 copy.37
  470.2 6.5 %fusion.63 = bf16[1,384,1536]{1,2,0:T(8,128)(2,1)S(1)} fusion(bf16[2048,384]{1,0:T(8,128)(2,1)S(1)} %bitcast.147, bf16[2048,3,1536]{2,0,1:T(8,128)(2,1)} %all-gather.5.cloned.1.call-done, bf16[2048]{0:T(1024)(128)(2,1)S(1)} %get-tuple-element.31), kind=kOutput, calls=%fused_computation.50 | convolution fusion | flops 2419654656 | bytes 9048064 | tf_op jit(solution)/shard_map/dot_general | solution.py:36
  476.8 6.7 %fusion.69 = bf16[1,384,1536]{1,2,0:T(8,128)(2,1)S(1)} fusion(bf16[2048,384]{1,0:T(8,128)(2,1)S(1)} %bitcast.148, bf16[2048,3,1536]{2,0,1:T(8,128)(2,1)} %all-gather.5.cloned.1.call-done, bf16[2048]{0:T(1024)(128)(2,1)S(1)} %get-tuple-element.32), kind=kOutput, calls=%fused_computation.52 | convolution fusion | flops 2419654656 | bytes 9048064 | tf_op jit(solution)/shard_map/dot_general | solution.py:36
  483.5 0.3 pad_maximum_fusion
  483.9 1.1 copy-done.6
  485.0 3.7 fusion.60
  488.6 3.9 fusion.66
  492.6 1.7 pad_maximum_fusion.1
  494.2 0.2 copy-done.4
  494.4 3.7 fusion.54
  498.1 4.7 fusion.57
  502.8 41.4 %reduce-scatter.8.cloned.1.call-done = f32[1,256,384]{2,1,0:T(8,128)} async-done(((f32[8,256,384]{2,1,0:T(8,128)}), f32[1,256,384]{2,1,0:T(8,128)}) %reduce-scatter.8.cloned.1.call-update) | async-done | bytes 393232 | tf_op jit(solution)/shard_map/reduce_scatter | solution.py:111
  544.2 1.7 dynamic-slice_bitcast_fusion.1
  545.9 6.2 %collective-permute-start = (bf16[128,384]{1,0:T(8,128)(2,1)}, bf16[128,384]{1,0:T(8,128)(2,1)}, u32[]{:S(2)}, u32[]{:S(2)}) collective-permute-start(bf16[128,384]{1,0:T(8,128)(2,1)} %get-tuple-element.25), channel_id=1, source_target_pairs={{0,0},{1,32},{2,64},{3,96},{4,8},{5,40},{6,72},{7,104},{8,16},{9,4... | collective-permute-start | bytes 294920 | tf_op jit(solution)/shard_map/ppermute | solution.py:119
  552.1 5.3 collective-permute-start.1
  557.4 2.9 pad_maximum_fusion.2
  560.4 2.6 copy.38
  563.0 4.3 copy.39
  567.2 1.0 select_convert_fusion.1
  568.2 0.7 pad_maximum_fusion.4
  (51 shorter events, 0.8 us)
Async XLA Ops:
  7.2 8.9 %copy-start = (s32[16]{0:T(128)S(1)}, s32[16]{0:T(128)}, u32[]{:S(2)}) copy-start(s32[16]{0:T(128)} %param.18) | copy-start | bytes 196
  9.8 6.3 %copy-start.9 = (s32[16]{0:T(128)S(1)}, s32[16]{0:T(128)}, u32[]{:S(2)}) copy-start(s32[16]{0:T(128)} %constant.52) | copy-start | bytes 196
  9.8 27.6 %all-to-all-start = ((bf16[128,16,384]{0,2,1:T(8,128)(2,1)}), bf16[128,16,384]{0,2,1:T(8,128)(2,1)S(1)}, u32[]{:S(2)}, u32[]{:S(2)}) async-start(bf16[128,16,384]{0,2,1:T(8,128)(2,1)} %bitcast.2), calls=%async_computation | async-start | bytes 3145728 | tf_op jit(solution)/shard_map/all_to_all | solution.py:64
  16.0 59.6 %reduce-scatter.4.cloned.1.call-start = ((), (), s32[]{:S(2)}) async-start(), calls=%async_computation.5 | async-start | bytes 18874368 | tf_op jit(solution)/shard_map/reduce_scatter | solution.py:80
  38.8 1.7 copy-start.2
  50.5 157.4 %reduce-scatter.6.cloned.1.call-start = ((), (), s32[]{:S(2)}) async-start(), calls=%async_computation.6 | async-start | bytes 7077888 | tf_op jit(solution)/shard_map/reduce_scatter | solution.py:83
  75.6 132.3 %copy-start.7 = (bf16[128,1536]{1,0:T(8,128)(2,1)S(1)}, bf16[128,1536]{1,0:T(8,128)(2,1)}, u32[]{:S(2)}) copy-start(bf16[128,1536]{1,0:T(8,128)(2,1)} %param.12) | copy-start | bytes 1179652
  75.6 132.3 %copy-start.8 = (bf16[128,1536]{1,0:T(8,128)(2,1)S(1)}, bf16[128,1536]{1,0:T(8,128)(2,1)}, u32[]{:S(2)}) copy-start(bf16[128,1536]{1,0:T(8,128)(2,1)} %param.13) | copy-start | bytes 1179652
  75.7 324.2 %all-gather.3.cloned.1.call-start = ((), (), s32[]{:S(2)}) async-start(), calls=%async_computation.7 | async-start | bytes 10616832 | tf_op jit(solution)/shard_map/all_gather | solution.py:89
  210.8 228.1 %all-gather.5.cloned.1.call-start = ((), (), s32[]{:S(2)}) async-start(), calls=%async_computation.8 | async-start | bytes 28311552 | tf_op jit(solution)/shard_map/all_gather | solution.py:90
  399.9 1.4 copy-start.3
  402.9 64.0 %all-to-all-start.1 = ((bf16[128,16,384]{0,2,1:T(8,128)(2,1)}), bf16[128,16,384]{0,2,1:T(8,128)(2,1)S(1)}, u32[]{:S(2)}, u32[]{:S(2)}) async-start(bf16[128,16,384]{0,2,1:T(8,128)(2,1)} %bitcast.142), calls=%async_computation.4 | async-start | bytes 3145728 | tf_op jit(solution)/shard_map/all_to_all | solution.py:66
  410.0 134.2 %reduce-scatter.8.cloned.1.call-start = ((), (), s32[]{:S(2)}) async-start(), calls=%async_computation.9 | async-start | bytes 3538944 | tf_op jit(solution)/shard_map/reduce_scatter | solution.py:111
  438.9 9.7 %copy-start.10 = (bf16[2048,3,1536]{2,0,1:T(8,128)(2,1)S(1)}, bf16[2048,3,1536]{2,0,1:T(8,128)(2,1)}, u32[]{:S(2)}) copy-start(bf16[2048,3,1536]{2,0,1:T(8,128)(2,1)} %all-gather.5.cloned.1.call-done) | copy-start | bytes 56623108
  438.9 10.3 %copy-start.11 = (bf16[2,384,1536]{2,1,0:T(8,128)(2,1)S(1)}, bf16[2,384,1536]{2,1,0:T(8,128)(2,1)}, u32[]{:S(2)}) copy-start(bf16[2,384,1536]{2,1,0:T(8,128)(2,1)} %param.15) | copy-start | bytes 7077892
  449.2 5.2 copy-start.12
  468.5 1.7 copy-start.5
  470.2 13.6 %slice-start = ((s8[18874368]{0:T(1024)(128)(4,1)}), s8[4194304]{0:T(1024)(128)(4,1)S(1)}, s32[]{:S(2)}) async-start(s8[18874368]{0:T(1024)(128)(4,1)} %bitcast.152), calls=%async_computation.10 | async-start | bytes 8388608
  470.2 13.6 %slice-start.1 = ((s8[18874368]{0:T(1024)(128)(4,1)}), s8[4194304]{0:T(1024)(128)(4,1)S(1)}, s32[]{:S(2)}) async-start(s8[18874368]{0:T(1024)(128)(4,1)} %bitcast.152), calls=%async_computation.11 | async-start | bytes 8388608
  470.2 13.6 %slice-start.2 = ((s8[18874368]{0:T(1024)(128)(4,1)}), s8[4194304]{0:T(1024)(128)(4,1)S(1)}, s32[]{:S(2)}) async-start(s8[18874368]{0:T(1024)(128)(4,1)} %bitcast.152), calls=%async_computation.12 | async-start | bytes 8388608
  476.8 7.1 %slice-start.3 = ((s8[18874368]{0:T(1024)(128)(4,1)}), s8[4194304]{0:T(1024)(128)(4,1)S(1)}, s32[]{:S(2)}) async-start(s8[18874368]{0:T(1024)(128)(4,1)} %bitcast.152), calls=%async_computation.13 | async-start | bytes 8388608
  476.8 7.1 %slice-start.4 = ((s8[18874368]{0:T(1024)(128)(4,1)}), s8[2097152]{0:T(1024)(128)(4,1)S(1)}, s32[]{:S(2)}) async-start(s8[18874368]{0:T(1024)(128)(4,1)} %bitcast.152), calls=%async_computation.14 | async-start | bytes 4194304
  483.5 1.4 copy-start.6
  492.5 1.9 copy-start.4
  545.9 21.3 %collective-permute-start = (bf16[128,384]{1,0:T(8,128)(2,1)}, bf16[128,384]{1,0:T(8,128)(2,1)}, u32[]{:S(2)}, u32[]{:S(2)}) collective-permute-start(bf16[128,384]{1,0:T(8,128)(2,1)} %get-tuple-element.25), channel_id=1, source_target_pairs={{0,0},{1,32},{2,64},{3,96},{4,8},{5,40},{6,72},{7,104},{8,16},{9,4... | collective-permute-start | bytes 294920 | tf_op jit(solution)/shard_map/ppermute | solution.py:119
  552.1 15.1 %collective-permute-start.1 = (bf16[128,384]{1,0:T(8,128)(2,1)}, bf16[128,384]{1,0:T(8,128)(2,1)}, u32[]{:S(2)}, u32[]{:S(2)}) collective-permute-start(bf16[128,384]{1,0:T(8,128)(2,1)} %get-tuple-element.26), channel_id=1, source_target_pairs={{0,16},{1,48},{2,80},{3,112},{4,24},{5,56},{6,88},{7,120},{8,0},{9... | collective-permute-start | bytes 294920 | tf_op jit(solution)/shard_map/ppermute | solution.py:119
  560.4 8.5 %copy-start.1 = (s32[16]{0:T(128)S(1)}, s32[16]{0:T(128)}, u32[]{:S(2)}) copy-start(s32[16]{0:T(128)} %param.18) | copy-start | bytes 196
Sparse Core Ops, SparseCore 0:
  50.6 24.9 reduce-scatter.3
  78.0 129.8 reduce-scatter.5
  210.9 188.9 all-gather.2
  401.4 37.4 all-gather.4
  467.0 77.1 reduce-scatter.7
where the time goes:
time: 582 us; the launch traced here: 576 us
  waiting for transfers between devices  436 us (75%)
  matrix products  65.2 us (11%)
  starting transfers between devices  25.5 us (4%)
  local copies, waits for them, and re-layouts  24.6 us (4%)
  between operations  15 us (3%)
  other arithmetic  9.76 us (2%)
    all_gather x1, waiting for transfers between devices, shards(): packed = lax.all_gather(packed, CHIPS, axis=0, tiled=True)  189 us
    reduce_scatter x1, waiting for transfers between devices, shards(): lax.psum_scatter(result, CHIPS, scatter_dimension=0, tiled=True)  132 us
    reduce_scatter x1, waiting for transfers between devices, shards(): lax.psum_scatter(partial_rows.reshape(N_TP, row_count // N_TP, width), TP...  41.4 us
    dot_general x6, matrix products, contract_cols(): lax.dot_general(left_op, right_op, (((1,), (1,)), ((), ())), preferred_el...  36 us
    dot_general x6, matrix products, contract_rows(): lax.dot_general(left_op, right_op, (((0,), (0,)), ((), ())), preferred_el...  29.2 us
    all_gather x1, waiting for transfers between devices, shards(): packed = lax.all_gather(packed, 'core', axis=0, tiled=True)  28.3 us
    reduce_scatter x1, waiting for transfers between devices, shards(): lax.psum_scatter(result.reshape(2, row_count // 2, ff), 'core', scatter_d...  25.1 us
    all_to_all x1, waiting for transfers between devices, shards(): lax.all_to_all(out_grad, DP, split_axis=1, concat_axis=0, tiled=True)  20.2 us
  transfers between devices with their start and end apart: 9, of which 6 were waited for; matrix products, arithmetic and copies ran while one was open for 13% of the time, Pallas kernels for 0%

commit v1 on v0

--- a/solution.py
+++ b/solution.py
@@ -13,6 +13,11 @@
 CHIPS = ("x", "ylo")
 N_DP = 16
 N_TP = 8
+
+
+def gather_over(x, name, dim):
+    stack = jnp.stack([x] * lax.axis_size(name))
+    return jnp.concatenate(lax.all_to_all(stack, name, 0, 0), axis=dim)
 
 
 def rank_of_pos(pos):
@@ -86,7 +91,7 @@
         hidden_grad * up_vals * sigmoid * (1.0 + gate_vals * (1.0 - sigmoid)) * row_mask
     ).astype(jnp.bfloat16)
     packed = jnp.stack([hidden, gate_grad, up_grad], axis=1)
-    packed = lax.all_gather(packed, CHIPS, axis=0, tiled=True)
+    packed = gather_over(packed, CHIPS, 0)
     packed = lax.all_gather(packed, "core", axis=0, tiled=True)
     hid_g, gate_g, up_g = (packed[:, 0], packed[:, 1], packed[:, 2])
     down_terms = []

time: 582 us -> 510 us (0.88)
  waiting for transfers between devices: 436 us -> 246 us
  blocking collectives: 0 us -> 110 us
  local copies, waits for them, and re-layouts: 24.6 us -> 33.8 us
    all_gather x1 -> x0, waiting for transfers between devices: 189 us -> none  [shards(): packed = lax.all_gather(packed, CHIPS, axis=0, tiled=True)]
    all_to_all x0 -> x1, blocking collectives: none -> 110 us  [gather_over(): return jnp.concatenate(lax.all_to_all(stack, name, 0, 0), axis=dim)]
    all_to_all x0 -> x1, local copies, waits for them, and re-layouts: none -> 8.25 us  [gather_over(): return jnp.concatenate(lax.all_to_all(stack, name, 0, 0), axis=dim)]
  transfers between devices with their start and end apart: 9 -> 8, of which waited for: 6 -> 5; matrix products, arithmetic and copies ran while one was open for 13% -> 14% of each run, Pallas kernels for 0% -> 0%
where the time goes in v1:
time: 510 us; the launch traced here: 503 us
  waiting for transfers between devices  246 us (48%)
  blocking collectives  110 us (22%)
  matrix products  65.1 us (13%)
  local copies, waits for them, and re-layouts  33.8 us (7%)
  starting transfers between devices  23.8 us (5%)
  between operations  15 us (3%)
  other arithmetic  8.75 us (2%)
    reduce_scatter x1, waiting for transfers between devices, shards(): lax.psum_scatter(result, CHIPS, scatter_dimension=0, tiled=True)  132 us
    all_to_all x1, blocking collectives, gather_over(): return jnp.concatenate(lax.all_to_all(stack, name, 0, 0), axis=dim)  110 us
    reduce_scatter x1, waiting for transfers between devices, shards(): lax.psum_scatter(partial_rows.reshape(N_TP, row_count // N_TP, width), TP...  41.8 us
    dot_general x6, matrix products, contract_cols(): lax.dot_general(left_op, right_op, (((1,), (1,)), ((), ())), preferred_el...  36.3 us
    dot_general x6, matrix products, contract_rows(): lax.dot_general(left_op, right_op, (((0,), (0,)), ((), ())), preferred_el...  28.8 us
    all_gather x1, waiting for transfers between devices, shards(): packed = lax.all_gather(packed, 'core', axis=0, tiled=True)  27.3 us
    reduce_scatter x1, waiting for transfers between devices, shards(): lax.psum_scatter(result.reshape(2, row_count // 2, ff), 'core', scatter_d...  25.1 us
    all_to_all x1, waiting for transfers between devices, shards(): lax.all_to_all(out_grad, DP, split_axis=1, concat_axis=0, tiled=True)  20.2 us
  transfers between devices with their start and end apart: 8, of which 5 were waited for; matrix products, arithmetic and copies ran while one was open for 14% of the time, Pallas kernels for 0%

profile of v1, /device:TPU:57, one launch (start us, length us, event | category | flops | bytes accessed | tf_op | source)
XLA Modules:
  0.0 502.8 jit_solution(12384394916500405793)
XLA Ops:
  7.2 2.6 copy.41
  9.8 6.2 %all-to-all-start = ((bf16[128,16,384]{0,2,1:T(8,128)(2,1)}), bf16[128,16,384]{0,2,1:T(8,128)(2,1)S(1)}, u32[]{:S(2)}, u32[]{:S(2)}) async-start(bf16[128,16,384]{0,2,1:T(8,128)(2,1)} %bitcast.2), calls=%async_computation | async-start | bytes 3145728 | tf_op jit(solution)/shard_map/all_to_all | solution.py:69
  16.1 0.7 gather_fusion
  17.2 20.2 %all-to-all-done = bf16[128,16,384]{0,2,1:T(8,128)(2,1)S(1)} async-done(((bf16[128,16,384]{0,2,1:T(8,128)(2,1)}), bf16[128,16,384]{0,2,1:T(8,128)(2,1)S(1)}, u32[]{:S(2)}, u32[]{:S(2)}) %all-to-all-start) | async-done | bytes 1572896 | tf_op jit(solution)/shard_map/all_to_all | solution.py:69
  37.4 0.9 copy.42
  38.2 0.4 broadcast_multiply_fusion
  38.6 0.2 copy.44
  39.0 1.5 copy-done.2
  40.5 3.5 fusion.77
  43.9 6.7 %convolution_add_fusion = f32[2048,1536]{1,0:T(8,128)} fusion(f32[2048,1536]{1,0:T(8,128)S(1)} %fusion.77, bf16[2048,384]{1,0:T(8,128)(2,1)S(1)} %bitcast.140, bf16[2,1536,384]{2,1,0:T(8,128)(2,1)S(1)} %copy-done.2), kind=kOutput, calls=%fused_computation.1 | convolution fusion | flops 2419064832 | bytes 27918336 | tf_op jit(solution)/shard_map/dot_general | solution.py:47
  50.7 25.1 %reduce-scatter.4.cloned.1.call-done = f32[1,1024,1536]{2,1,0:T(8,128)} async-done(((f32[2,1024,1536]{2,1,0:T(8,128)}), f32[1,1024,1536]{2,1,0:T(8,128)}) %reduce-scatter.4.cloned.1.call-update) | async-done | bytes 6291472 | tf_op jit(solution)/shard_map/reduce_scatter | solution.py:85
  76.6 131.5 %reduce-scatter.6.cloned.1.call-done = f32[128,1536]{1,0:T(8,128)} async-done(((f32[1024,1536]{1,0:T(8,128)}), f32[128,1536]{1,0:T(8,128)}) %reduce-scatter.6.cloned.1.call-update) | async-done | bytes 786448 | tf_op jit(solution)/shard_map/reduce_scatter | solution.py:88
  208.1 1.7 fusion.97
  209.9 1.0 stack.63
  211.0 110.4 %all_to_all.37 = bf16[8,128,3,1536]{3,1,2,0:T(8,128)(2,1)} all-to-all(bf16[8,128,3,1536]{3,1,2,0:T(8,128)(2,1)S(1)} %stack.63), channel_id=1, replica_groups=mesh['x'=4,'ylo'=2,'core'=2,'z'=4,'yhi'=2] {'x','ylo'}, dimensions={0} | all-to-all | bytes 18874368 | tf_op jit(solution)/shard_map/all_to_all | solution.py:20
  321.3 8.3 %copy.47 = bf16[8,128,3,1536]{3,1,0,2:T(8,128)(2,1)} copy(bf16[8,128,3,1536]{3,1,2,0:T(8,128)(2,1)} %all_to_all.37) | data formatting | bytes 18874368 | tf_op jit(solution)/shard_map/all_to_all | solution.py:20
  329.6 1.4 copy-done.3
  331.0 1.6 copy.48
  332.6 5.5 %all-to-all-start.2 = ((bf16[128,16,384]{0,2,1:T(8,128)(2,1)}), bf16[128,16,384]{0,2,1:T(8,128)(2,1)S(1)}, u32[]{:S(2)}, u32[]{:S(2)}) async-start(bf16[128,16,384]{0,2,1:T(8,128)(2,1)} %bitcast.144), calls=%async_computation.5 | async-start | bytes 3145728 | tf_op jit(solution)/shard_map/all_to_all | solution.py:71
  338.1 0.5 reduce-scatter.8.cloned.1.call-start
  338.7 27.3 %all-gather.2.cloned.1.call-done = bf16[2048,3,1536]{2,0,1:T(8,128)(2,1)} async-done(((bf16[1024,3,1536]{2,0,1:T(8,128)(2,1)}), bf16[2048,3,1536]{2,0,1:T(8,128)(2,1)}) %all-gather.2.cloned.1.call-update) | async-done | bytes 18874384 | tf_op jit(solution)/shard_map/all_gather | solution.py:95
  366.1 8.4 %fusion.14 = f32[2048,384]{1,0:T(8,128)} fusion(bf16[2048,3,1536]{2,0,1:T(8,128)(2,1)} %all-gather.2.cloned.1.call-done, bf16[2048]{0:T(1024)(128)(2,1)S(1)} %broadcast_bitcast_fusion.1, bf16[2,384,1536]{2,1,0:T(8,128)(2,1)} %param.15), kind=kOutput, calls=%fused_computation.16 | convolution fusion | flops 2419064832 | bytes 10620928 | tf_op jit(solution)/shard_map/dot_general | solution.py:47
  374.5 1.2 copy-done.10
  375.7 0.7 copy-done.12
  376.4 5.2 %fusion.18 = f32[2048,384]{1,0:T(8,128)} fusion(bf16[2048,3,1536]{2,0,1:T(8,128)(2,1)S(1)} %copy-done.10, bf16[2048]{0:T(1024)(128)(2,1)S(1)} %broadcast_bitcast_fusion.1, bf16[2,384,1536]{2,1,0:T(8,128)(2,1)S(1)} %copy-done.12), kind=kOutput, calls=%fused_computation.20 | convolution fusion | flops 2419064832 | bytes 10620928 | tf_op jit(solution)/shard_map/dot_general | solution.py:47
  381.6 5.2 %fusion.6 = f32[2048,384]{1,0:T(8,128)} fusion(bf16[2048,3,1536]{2,0,1:T(8,128)(2,1)S(1)} %copy-done.10, bf16[2048]{0:T(1024)(128)(2,1)S(1)} %broadcast_bitcast_fusion, bf16[2,384,1536]{2,1,0:T(8,128)(2,1)S(1)} %copy-done.11), kind=kOutput, calls=%fused_computation.8 | convolution fusion | flops 2419064832 | bytes 10620928 | tf_op jit(solution)/shard_map/dot_general | solution.py:47
  386.8 7.3 %add_add_fusion = f32[2048,384]{1,0:T(8,128)} fusion(f32[2048,384]{1,0:T(8,128)} %fusion.6, f32[2048,384]{1,0:T(8,128)} %fusion.18, f32[2048,384]{1,0:T(8,128)} %fusion.14, bf16[2048,3,1536]{2,0,1:T(8,128)(2,1)S(1)} %copy-done.10, bf16[2048]{0:T(1024)(128)(2,1)S(1)} %broadcast_bitcast_fusion, bf16[2,384,1536]{2,1,0:T(8,128)(2,1)S(1)} %copy-done.12), kind=kOutput, calls=%fused_computation.30 | convolution fusion | flops 2421424128 | bytes 20058112 | tf_op jit(solution)/shard_map/dot_general | solution.py:47
  394.1 1.6 copy.50
  395.7 1.7 copy.51
  397.5 6.5 %fusion.60 = bf16[1,384,1536]{1,2,0:T(8,128)(2,1)S(1)} fusion(bf16[2048,384]{1,0:T(8,128)(2,1)S(1)} %bitcast.149, bf16[2048,3,1536]{2,0,1:T(8,128)(2,1)} %all-gather.2.cloned.1.call-done, bf16[2048]{0:T(1024)(128)(2,1)S(1)} %broadcast_bitcast_fusion), kind=kOutput, calls=%fused_computation.49 | convolution fusion | flops 2419654656 | bytes 9048064 | tf_op jit(solution)/shard_map/dot_general | solution.py:41
  404.0 6.7 %fusion.66 = bf16[1,384,1536]{1,2,0:T(8,128)(2,1)S(1)} fusion(bf16[2048,384]{1,0:T(8,128)(2,1)S(1)} %bitcast.150, bf16[2048,3,1536]{2,0,1:T(8,128)(2,1)} %all-gather.2.cloned.1.call-done, bf16[2048]{0:T(1024)(128)(2,1)S(1)} %broadcast_bitcast_fusion.1), kind=kOutput, calls=%fused_computation.51 | convolution fusion | flops 2419654656 | bytes 9048064 | tf_op jit(solution)/shard_map/dot_general | solution.py:41
  410.7 0.3 pad_maximum_fusion.1
  411.1 1.1 copy-done.6
  412.2 3.6 fusion.63
  415.7 3.8 fusion.69
  419.6 1.7 pad_maximum_fusion
  421.2 0.2 copy-done.4
  421.4 3.6 fusion.54
  425.0 4.6 fusion.57
  429.6 41.8 %reduce-scatter.8.cloned.1.call-done = f32[1,256,384]{2,1,0:T(8,128)} async-done(((f32[8,256,384]{2,1,0:T(8,128)}), f32[1,256,384]{2,1,0:T(8,128)}) %reduce-scatter.8.cloned.1.call-update) | async-done | bytes 393232 | tf_op jit(solution)/shard_map/reduce_scatter | solution.py:116
  471.4 1.7 dynamic-slice_bitcast_fusion.1
  473.1 6.2 %collective-permute-start = (bf16[128,384]{1,0:T(8,128)(2,1)}, bf16[128,384]{1,0:T(8,128)(2,1)}, u32[]{:S(2)}, u32[]{:S(2)}) collective-permute-start(bf16[128,384]{1,0:T(8,128)(2,1)} %get-tuple-element.29), channel_id=1, source_target_pairs={{0,0},{1,32},{2,64},{3,96},{4,8},{5,40},{6,72},{7,104},{8,16},{9,4... | collective-permute-start | bytes 294920 | tf_op jit(solution)/shard_map/ppermute | solution.py:124
  479.4 5.2 %collective-permute-start.1 = (bf16[128,384]{1,0:T(8,128)(2,1)}, bf16[128,384]{1,0:T(8,128)(2,1)}, u32[]{:S(2)}, u32[]{:S(2)}) collective-permute-start(bf16[128,384]{1,0:T(8,128)(2,1)} %get-tuple-element.30), channel_id=1, source_target_pairs={{0,16},{1,48},{2,80},{3,112},{4,24},{5,56},{6,88},{7,120},{8,0},{9... | collective-permute-start | bytes 294920 | tf_op jit(solution)/shard_map/ppermute | solution.py:124
  484.6 2.9 pad_maximum_fusion.2
  487.5 2.6 copy.53
  490.1 4.3 copy.52
  494.4 1.0 select_convert_fusion.1
  495.4 0.7 pad_maximum_fusion.4
  (52 shorter events, 1.1 us)
Async XLA Ops:
  7.2 8.9 %copy-start = (s32[16]{0:T(128)S(1)}, s32[16]{0:T(128)}, u32[]{:S(2)}) copy-start(s32[16]{0:T(128)} %param.18) | copy-start | bytes 196
  9.8 6.3 %copy-start.9 = (s32[16]{0:T(128)S(1)}, s32[16]{0:T(128)}, u32[]{:S(2)}) copy-start(s32[16]{0:T(128)} %constant.52) | copy-start | bytes 196
  9.8 27.6 %all-to-all-start = ((bf16[128,16,384]{0,2,1:T(8,128)(2,1)}), bf16[128,16,384]{0,2,1:T(8,128)(2,1)S(1)}, u32[]{:S(2)}, u32[]{:S(2)}) async-start(bf16[128,16,384]{0,2,1:T(8,128)(2,1)} %bitcast.2), calls=%async_computation | async-start | bytes 3145728 | tf_op jit(solution)/shard_map/all_to_all | solution.py:69
  16.0 59.8 %reduce-scatter.4.cloned.1.call-start = ((), (), s32[]{:S(2)}) async-start(), calls=%async_computation.6 | async-start | bytes 18874368 | tf_op jit(solution)/shard_map/reduce_scatter | solution.py:85
  38.8 1.7 copy-start.2
  50.6 157.4 %reduce-scatter.6.cloned.1.call-start = ((), (), s32[]{:S(2)}) async-start(), calls=%async_computation.7 | async-start | bytes 7077888 | tf_op jit(solution)/shard_map/reduce_scatter | solution.py:88
  75.8 132.3 %copy-start.7 = (bf16[128,1536]{1,0:T(8,128)(2,1)S(1)}, bf16[128,1536]{1,0:T(8,128)(2,1)}, u32[]{:S(2)}) copy-start(bf16[128,1536]{1,0:T(8,128)(2,1)} %param.12) | copy-start | bytes 1179652
  75.8 132.3 %copy-start.8 = (bf16[128,1536]{1,0:T(8,128)(2,1)S(1)}, bf16[128,1536]{1,0:T(8,128)(2,1)}, u32[]{:S(2)}) copy-start(bf16[128,1536]{1,0:T(8,128)(2,1)} %param.13) | copy-start | bytes 1179652
  75.8 290.3 %all-gather.2.cloned.1.call-start = ((), (), s32[]{:S(2)}) async-start(), calls=%async_computation.8 | async-start | bytes 28311552 | tf_op jit(solution)/shard_map/all_gather | solution.py:95
  329.6 1.4 copy-start.3
  332.6 61.6 %all-to-all-start.2 = ((bf16[128,16,384]{0,2,1:T(8,128)(2,1)}), bf16[128,16,384]{0,2,1:T(8,128)(2,1)S(1)}, u32[]{:S(2)}, u32[]{:S(2)}) async-start(bf16[128,16,384]{0,2,1:T(8,128)(2,1)} %bitcast.144), calls=%async_computation.5 | async-start | bytes 3145728 | tf_op jit(solution)/shard_map/all_to_all | solution.py:71
  338.1 133.3 %reduce-scatter.8.cloned.1.call-start = ((), (), s32[]{:S(2)}) async-start(), calls=%async_computation.9 | async-start | bytes 3538944 | tf_op jit(solution)/shard_map/reduce_scatter | solution.py:116
  366.1 9.7 %copy-start.10 = (bf16[2048,3,1536]{2,0,1:T(8,128)(2,1)S(1)}, bf16[2048,3,1536]{2,0,1:T(8,128)(2,1)}, u32[]{:S(2)}) copy-start(bf16[2048,3,1536]{2,0,1:T(8,128)(2,1)} %all-gather.2.cloned.1.call-done) | copy-start | bytes 56623108
  366.1 10.3 %copy-start.12 = (bf16[2,384,1536]{2,1,0:T(8,128)(2,1)S(1)}, bf16[2,384,1536]{2,1,0:T(8,128)(2,1)}, u32[]{:S(2)}) copy-start(bf16[2,384,1536]{2,1,0:T(8,128)(2,1)} %param.14) | copy-start | bytes 7077892
  376.4 5.2 %copy-start.11 = (bf16[2,384,1536]{2,1,0:T(8,128)(2,1)S(1)}, bf16[2,384,1536]{2,1,0:T(8,128)(2,1)}, u32[]{:S(2)}) copy-start(bf16[2,384,1536]{2,1,0:T(8,128)(2,1)} %param.15) | copy-start | bytes 7077892
  395.7 1.7 copy-start.5
  397.4 13.6 %slice-start = ((s8[18874368]{0:T(1024)(128)(4,1)}), s8[4194304]{0:T(1024)(128)(4,1)S(1)}, s32[]{:S(2)}) async-start(s8[18874368]{0:T(1024)(128)(4,1)} %bitcast.154), calls=%async_computation.10 | async-start | bytes 8388608
  397.4 13.6 %slice-start.1 = ((s8[18874368]{0:T(1024)(128)(4,1)}), s8[4194304]{0:T(1024)(128)(4,1)S(1)}, s32[]{:S(2)}) async-start(s8[18874368]{0:T(1024)(128)(4,1)} %bitcast.154), calls=%async_computation.11 | async-start | bytes 8388608
  397.5 13.6 %slice-start.2 = ((s8[18874368]{0:T(1024)(128)(4,1)}), s8[4194304]{0:T(1024)(128)(4,1)S(1)}, s32[]{:S(2)}) async-start(s8[18874368]{0:T(1024)(128)(4,1)} %bitcast.154), calls=%async_computation.12 | async-start | bytes 8388608
  404.0 7.1 %slice-start.3 = ((s8[18874368]{0:T(1024)(128)(4,1)}), s8[4194304]{0:T(1024)(128)(4,1)S(1)}, s32[]{:S(2)}) async-start(s8[18874368]{0:T(1024)(128)(4,1)} %bitcast.154), calls=%async_computation.13 | async-start | bytes 8388608
  404.0 7.1 %slice-start.4 = ((s8[18874368]{0:T(1024)(128)(4,1)}), s8[2097152]{0:T(1024)(128)(4,1)S(1)}, s32[]{:S(2)}) async-start(s8[18874368]{0:T(1024)(128)(4,1)} %bitcast.154), calls=%async_computation.14 | async-start | bytes 4194304
  410.7 1.4 copy-start.6
  419.5 1.9 copy-start.4
  473.1 21.3 %collective-permute-start = (bf16[128,384]{1,0:T(8,128)(2,1)}, bf16[128,384]{1,0:T(8,128)(2,1)}, u32[]{:S(2)}, u32[]{:S(2)}) collective-permute-start(bf16[128,384]{1,0:T(8,128)(2,1)} %get-tuple-element.29), channel_id=1, source_target_pairs={{0,0},{1,32},{2,64},{3,96},{4,8},{5,40},{6,72},{7,104},{8,16},{9,4... | collective-permute-start | bytes 294920 | tf_op jit(solution)/shard_map/ppermute | solution.py:124
  479.4 15.0 %collective-permute-start.1 = (bf16[128,384]{1,0:T(8,128)(2,1)}, bf16[128,384]{1,0:T(8,128)(2,1)}, u32[]{:S(2)}, u32[]{:S(2)}) collective-permute-start(bf16[128,384]{1,0:T(8,128)(2,1)} %get-tuple-element.30), channel_id=1, source_target_pairs={{0,16},{1,48},{2,80},{3,112},{4,24},{5,56},{6,88},{7,120},{8,0},{9... | collective-permute-start | bytes 294920 | tf_op jit(solution)/shard_map/ppermute | solution.py:124
  487.5 8.5 %copy-start.1 = (s32[16]{0:T(128)S(1)}, s32[16]{0:T(128)}, u32[]{:S(2)}) copy-start(s32[16]{0:T(128)} %param.18) | copy-start | bytes 196
Sparse Core Ops, SparseCore 0:
  50.8 24.9 reduce-scatter.3
  78.2 129.8 reduce-scatter.5
  329.8 36.2 all-gather.1
  394.2 77.1 reduce-scatter.7
